TPU v7x, 256 devices: a whole 4x4x8 slice. The times are simulated.
256 devices in a mesh: in: 4 (over x), out: 64 (over z, y, core).
Axes of the slice: x: 4, y: 4, z: 8, core: 2. Of those that a mesh axis runs over, the one named last changes fastest.
Arguments:
- activations: bfloat16 [8192, 4096], P('out', 'in'), may hold values from -6 to 6
- out_grad: bfloat16 [8192, 16384], P('in', 'out'), may hold values from -0.06591797 to 0.06591797
- block_rows: int32 [4, 64, 4], P('in', 'out'), may hold values from 0 to 31, as said below
- block_cols: int32 [4, 64, 4], P('in', 'out'), may hold values from 0 to 127, as said below
- counts: int32 [4, 64], P('in', 'out'), may hold values from 1 to 4, as said below
Outputs:
- grad_blocks: float32 [4, 64, 4, 128, 128], P('in', 'out')
Inputs may be any that keep to these rules, and one draw needn't show every extreme that they name: `block_rows`: tile (i, j) lists blocks of its own region only: rows i * 8 to (i + 1) * 8 - 1; slots of one tile name different blocks, and slots past counts[i, j] also name blocks of the tile. `block_cols`: columns j * 2 to (j + 1) * 2 - 1 for tile (i, j). `counts`: some tile has a full list in every draw.
All inputs are finite; a program needn't handle non-finite values.
Results may differ from a plain program's by a relative error of at most 0.0003.
Values may be sent and summed in bfloat16 or wider, within the bound.
No kernel may reach another device: no remote copies, remote signals or barrier semaphores. Data moves between devices by JAX's collectives and lax.ppermute only.
A program may use at most 128 MiB of HBM per device.

v0:
```python
import jax
import jax.numpy as jnp
from jax import lax
from jax.sharding import PartitionSpec as P

BLK = 128
MAXB = 4


def block_products(left_rows, grad_rows, local_cols, tile_cols):
    width = grad_rows.shape[0]
    right = jnp.take(grad_rows.reshape(width, tile_cols, BLK), local_cols, axis=1)
    return jnp.einsum("nbi,nbj->bij", left_rows, right, preferred_element_type=jnp.float32)


def on_device(activations, out_grad, block_rows, block_cols, counts):
    in_place = lax.axis_index("in")
    out_place = lax.axis_index("out")
    tile_rows = activations.shape[1] // BLK
    tile_cols = out_grad.shape[1] // BLK
    local_rows = block_rows[0, 0] - in_place * tile_rows
    local_cols = block_cols[0, 0] - out_place * tile_cols
    live = counts[0, 0]
    grad_all = lax.all_gather(out_grad, "in", axis=0, tiled=True)
    piece = lax.all_gather(activations, "out", axis=0, tiled=True)
    height = piece.shape[0]
    left = jnp.take(piece.reshape(height, tile_rows, BLK), local_rows, axis=1)
    totals = block_products(left, grad_all, local_cols, tile_cols)
    keep = (jnp.arange(MAXB, dtype=jnp.int32) < live)[:, None, None]
    result = jnp.where(keep, totals, jnp.zeros_like(totals))
    return result.reshape(1, 1, MAXB, BLK, BLK)


def solution(mesh):
    return jax.shard_map(
        on_device,
        mesh=mesh,
        in_specs=(
            P("out", "in"),
            P("in", "out"),
            P("in", "out", None),
            P("in", "out", None),
            P("in", "out"),
        ),
        out_specs=P("in", "out", None, None, None),
        check_vma=False,
    )
```

profile of v0, /device:TPU:1, one launch (start us, length us, event | category | flops | bytes accessed | tf_op | source)
XLA Modules:
  0.0 228.5 jit_solution(16223086437838721816)
XLA Ops:
  6.5 0.0 all-gather.5.cloned.1.call-start
  6.5 0.7 all-gather.5.cloned.1.call-update
  7.3 0.0 all-gather.3.cloned.1.call-start
  7.3 0.7 all-gather.3.cloned.1.call-update
  8.7 0.7 fusion.11
  9.3 0.7 fusion.10
  10.0 0.7 compare_and_fusion
  10.7 52.8 %all-gather.5.cloned.1.call-done = bf16[8192,256]{1,0:T(8,128)(2,1)} async-done(((bf16[2048,256]{1,0:T(8,128)(2,1)}), bf16[8192,256]{1,0:T(8,128)(2,1)}) %all-gather.5.cloned.1.call-update) | async-done | bytes 4194320 | tf_op jit(solution)/shard_map/all_gather | solution.py:24
  63.5 4.5 %fusion.15 = (bf16[4096,256]{1,0:T(8,128)(2,1)}, bf16[4096,256]{1,0:T(8,128)(2,1)}) fusion(bf16[8192,256]{1,0:T(8,128)(2,1)} %all-gather.5.cloned.1.call-done), kind=kLoop, calls=%fused_computation.30 | loop fusion | bytes 8388608 | tf_op jit(solution)/shard_map/jit(_take)/gather | solution.py:12
  68.0 2.9 %copy.9 = bf16[4096,256]{0,1:T(8,128)(2,1)S(1)} copy(bf16[4096,256]{1,0:T(8,128)(2,1)} %get-tuple-element.7) | data formatting | bytes 4194304 | tf_op jit(solution)/shard_map/jit(_take)/gather | solution.py:12
  70.9 4.1 %copy.10 = bf16[4096,256]{0,1:T(8,128)(2,1)} copy(bf16[4096,256]{1,0:T(8,128)(2,1)} %get-tuple-element.8) | data formatting | bytes 4194304 | tf_op jit(solution)/shard_map/jit(_take)/gather | solution.py:12
  75.0 2.8 %gather_fusion.2 = bf16[4,4096,128]{1,2,0:T(8,128)(2,1)} fusion(bf16[4096,2,128]{0,2,1:T(8,128)(2,1)S(1)} %bitcast.26, s32[1024]{0:T(1024)S(1)} %pad_clamp_fusion), kind=kCustom, calls=%fused_computation.2 | custom fusion | bytes 8388624 | tf_op jit(solution)/shard_map/jit(_take)/gather | solution.py:12
  77.8 4.6 %gather_fusion.3 = bf16[4,4096,128]{1,2,0:T(8,128)(2,1)} fusion(bf16[4096,2,128]{0,2,1:T(8,128)(2,1)} %bitcast.27, s32[1024]{0:T(1024)S(1)} %pad_clamp_fusion), kind=kCustom, calls=%fused_computation.3 | custom fusion | bytes 8388624 | tf_op jit(solution)/shard_map/jit(_take)/gather | solution.py:12
  82.4 84.2 %all-gather.3.cloned.1.call-done = bf16[8192,1024]{1,0:T(8,128)(2,1)} async-done(((bf16[128,1024]{1,0:T(8,128)(2,1)}), bf16[8192,1024]{1,0:T(8,128)(2,1)}) %all-gather.3.cloned.1.call-update) | async-done | bytes 16777232 | tf_op jit(solution)/shard_map/all_gather | solution.py:25
  166.5 11.6 %fusion.14 = (bf16[4096,1024]{1,0:T(8,128)(2,1)}, bf16[4096,1024]{1,0:T(8,128)(2,1)}) fusion(bf16[8192,1024]{1,0:T(8,128)(2,1)} %all-gather.3.cloned.1.call-done), kind=kLoop, calls=%fused_computation.29 | loop fusion | bytes 33554432 | tf_op jit(solution)/shard_map/jit(_take)/gather | solution.py:27
  178.2 11.3 %copy.7 = bf16[4096,1024]{0,1:T(8,128)(2,1)} copy(bf16[4096,1024]{1,0:T(8,128)(2,1)} %get-tuple-element.5) | data formatting | bytes 16777216 | tf_op jit(solution)/shard_map/jit(_take)/gather | solution.py:27
  189.5 11.8 %copy.8 = bf16[4096,1024]{0,1:T(8,128)(2,1)} copy(bf16[4096,1024]{1,0:T(8,128)(2,1)} %get-tuple-element.6) | data formatting | bytes 16777216 | tf_op jit(solution)/shard_map/jit(_take)/gather | solution.py:27
  201.3 6.1 %gather_fusion = bf16[4,4096,128]{1,2,0:T(8,128)(2,1)} fusion(bf16[4096,8,128]{0,2,1:T(8,128)(2,1)} %bitcast.24, s32[1024]{0:T(1024)S(1)} %pad_clamp_fusion.1), kind=kCustom, calls=%fused_computation | custom fusion | bytes 8388624 | tf_op jit(solution)/shard_map/jit(_take)/gather | solution.py:27
  207.4 6.2 %gather_fusion.1 = bf16[4,4096,128]{1,2,0:T(8,128)(2,1)} fusion(bf16[4096,8,128]{0,2,1:T(8,128)(2,1)} %bitcast.25, s32[1024]{0:T(1024)S(1)} %pad_clamp_fusion.1), kind=kCustom, calls=%fused_computation.1 | custom fusion | bytes 8388624 | tf_op jit(solution)/shard_map/jit(_take)/gather | solution.py:27
  213.6 8.1 %fusion.9 = f32[1,1,4,128,128]{4,3,2,1,0:T(8,128)} fusion(bf16[4096,4,128]{0,2,1:T(8,128)(2,1)} %bitcast.29, bf16[4096,4,128]{0,2,1:T(8,128)(2,1)} %bitcast.28, pred[4]{0:T(512)(128)(4,1)S(1)} %get-tuple-element.9, bf16[4096,4,128]{0,2,1:T(8,128)(2,1)} %bitcast.31, bf16[4096,4,128]{0,2,1:T(8,128)(2,1)} %bitcast.30, pred[4]{0:T(512)(128)(4,1)S(1)} %get-tuple-element.10, ...), kind=kOutput, calls=%fused_computation.15 | convolution fusion | flops 1115750400 | bytes 17039372 | tf_op jit(solution)/shard_map/nbi,nbj->bij/dot_general | solution.py:13
  (3 shorter events, 0.0 us)
Async XLA Ops:
  6.5 57.0 %all-gather.5.cloned.1.call-start = ((), (), s32[]{:S(2)}) async-start(), calls=%async_computation.1 | async-start | bytes 5242880 | tf_op jit(solution)/shard_map/all_gather | solution.py:24
  7.3 159.3 %all-gather.3.cloned.1.call-start = ((), (), s32[]{:S(2)}) async-start(), calls=%async_computation | async-start | bytes 17039360 | tf_op jit(solution)/shard_map/all_gather | solution.py:25
Sparse Core Ops, SparseCore 0:
  9.1 54.3 all-gather.4
  66.3 100.2 all-gather.2
where the time goes:
time: 229 us
  waiting for transfers between devices  138 us (60%)
  local copies, waits for them, and re-layouts  65.8 us (29%)
  between operations  14.1 us (6%)
  matrix products  8.1 us (4%)
    all_gather x1, waiting for transfers between devices, on_device(): piece = lax.all_gather(activations, 'out', axis=0, tiled=True)  84.2 us
    all_gather x1, waiting for transfers between devices, on_device(): grad_all = lax.all_gather(out_grad, 'in', axis=0, tiled=True)  52.8 us
    gather x5, local copies, waits for them, and re-layouts, on_device(): left = jnp.take(piece.reshape(height, tile_rows, BLK), local_rows, axis=1)  47 us
    gather x5, local copies, waits for them, and re-layouts, block_products(): jnp.take(grad_rows.reshape(width, tile_cols, BLK), local_cols, axis=1)  18.8 us
    dot_general x1, matrix products, block_products(): jnp.einsum('nbi,nbj->bij', left_rows, right, preferred_element_type=jnp.f...  8.1 us
  transfers between devices with their start and end apart: 2, of which 2 were waited for; matrix products, arithmetic and copies ran while one was open for 9% of the time, Pallas kernels for 0%

commit v1 on v0

v1 whole, which is shorter than its diff:
```python
import functools

import jax
import jax.numpy as jnp
from jax import lax
from jax.experimental import pallas as pl
from jax.experimental.pallas import tpu as pltpu
from jax.sharding import PartitionSpec as P

BLK = 128
MAXB = 4
CHUNK = 512


def block_kernel(n_grad, rows_ref, cols_ref, live_ref, starts_ref, act_hbm, *rest):
    grad_hbm = rest[:n_grad]
    out_ref, a_v, g_v, sems = rest[n_grad:]
    tokens = a_v.shape[1]

    copies = []
    for s in range(MAXB):
        r = pl.multiple_of(rows_ref[s] * BLK, BLK)
        c = pl.multiple_of(cols_ref[s] * BLK, BLK)
        slot = [pltpu.make_async_copy(act_hbm.at[:, pl.ds(r, BLK)], a_v.at[s], sems.at[s, 0])]
        for p, piece in enumerate(grad_hbm):
            length = piece.shape[0]
            slot.append(
                pltpu.make_async_copy(
                    piece.at[:, pl.ds(c, BLK)],
                    g_v.at[s, pl.ds(pl.multiple_of(starts_ref[p], BLK), length)],
                    sems.at[s, p + 1],
                )
            )
        for cp in slot:
            cp.start()
        copies.append(slot)

    live = live_ref[0]
    for s in range(MAXB):
        for cp in copies[s]:
            cp.wait()

        def body(k, acc):
            t = pl.multiple_of(k * CHUNK, CHUNK)
            a = a_v[s, pl.ds(t, CHUNK), :]
            g = g_v[s, pl.ds(t, CHUNK), :]
            return acc + lax.dot_general(
                a, g, (((0,), (0,)), ((), ())), preferred_element_type=jnp.float32
            )

        acc = lax.fori_loop(0, tokens // CHUNK, body, jnp.zeros((BLK, BLK), jnp.float32))
        out_ref[s] = jnp.where(s < live, acc, jnp.zeros_like(acc))


def block_products(act_all, grad_pieces, starts, local_rows, local_cols, live):
    tokens = act_all.shape[0]
    n_grad = len(grad_pieces)
    smem = pl.BlockSpec(memory_space=pltpu.SMEM)
    hbm = pl.BlockSpec(memory_space=pl.ANY)
    flops = 2 * MAXB * tokens * BLK * BLK
    moved = 2 * MAXB * tokens * BLK * 2 + MAXB * BLK * BLK * 4
    return pl.pallas_call(
        functools.partial(block_kernel, n_grad),
        out_shape=jax.ShapeDtypeStruct((MAXB, BLK, BLK), jnp.float32),
        in_specs=[smem, smem, smem, smem, hbm] + [hbm] * n_grad,
        out_specs=pl.BlockSpec(memory_space=pltpu.VMEM),
        scratch_shapes=[
            pltpu.VMEM((MAXB, tokens, BLK), jnp.bfloat16),
            pltpu.VMEM((MAXB, tokens, BLK), jnp.bfloat16),
            pltpu.SemaphoreType.DMA((MAXB, 1 + n_grad)),
        ],
        compiler_params=pltpu.CompilerParams(vmem_limit_bytes=48 * 1024 * 1024),
        cost_estimate=pl.CostEstimate(flops=flops, bytes_accessed=moved, transcendentals=0),
    )(local_rows, local_cols, live, starts, act_all, *grad_pieces)


def ring_gather(own, axis, place):
    n = lax.axis_size(axis)
    length = own.shape[0]
    right = [(k, (k + 1) % n) for k in range(n)]
    left = [(k, (k - 1) % n) for k in range(n)]
    pieces, starts = [own], [place * length]
    from_left, from_right = own, own
    for d in range(1, (n + 1) // 2):
        from_left = lax.ppermute(from_left, axis, right)
        from_right = lax.ppermute(from_right, axis, left)
        pieces += [from_left, from_right]
        starts += [((place - d) % n) * length, ((place + d) % n) * length]
    if n % 2 == 0 and n > 1:
        half = length // 2
        d = n // 2
        if d == 1:
            near_a, near_b = lax.ppermute(own[:half], axis, right), lax.ppermute(own[half:], axis, left)
        else:
            near_a = lax.ppermute(from_left[:half], axis, right)
            near_b = lax.ppermute(from_right[half:], axis, left)
        far = ((place + d) % n) * length
        pieces += [near_a, near_b]
        starts += [far, far + half]
    return pieces, jnp.stack(starts).astype(jnp.int32)


def on_device(activations, out_grad, block_rows, block_cols, counts):
    in_place = lax.axis_index("in")
    out_place = lax.axis_index("out")
    tile_rows = activations.shape[1] // BLK
    tile_cols = out_grad.shape[1] // BLK
    local_rows = jnp.clip(block_rows[0, 0] - in_place * tile_rows, 0, tile_rows - 1)
    local_cols = jnp.clip(block_cols[0, 0] - out_place * tile_cols, 0, tile_cols - 1)
    live = counts[0].astype(jnp.int32)
    act_all = lax.all_gather(activations, "out", axis=0, tiled=True)
    grad_pieces, starts = ring_gather(out_grad, "in", in_place)
    totals = block_products(act_all, grad_pieces, starts, local_rows, local_cols, live)
    return totals.reshape(1, 1, MAXB, BLK, BLK)


def solution(mesh):
    return jax.shard_map(
        on_device,
        mesh=mesh,
        in_specs=(
            P("out", "in"),
            P("in", "out"),
            P("in", "out", None),
            P("in", "out", None),
            P("in", "out"),
        ),
        out_specs=P("in", "out", None, None, None),
        check_vma=False,
    )
```

time: 229 us -> 140 us (0.61)
  local copies, waits for them, and re-layouts: 65.8 us -> 2.99 us
  waiting for transfers between devices: 138 us -> 97.1 us
  Pallas kernels: 0 us -> 17.9 us
  matrix products: 8.1 us -> 0 us
  starting transfers between devices: 0.04 us -> 6.83 us
    all_gather x2 -> x1, waiting for transfers between devices: 137 us -> 66.6 us  [on_device(): act_all = lax.all_gather(activations, 'out', axis=0, tiled=True)]
    gather x10 -> x0, local copies, waits for them, and re-layouts: 65.8 us -> none  [the longest x5 47 us: on_device(): left = jnp.take(piece.reshape(height, tile_rows, BLK), local_rows, axis=1)]
    ppermute x0 -> x4, waiting for transfers between devices: none -> 29.9 us  [the longest x1 20.9 us: ring_gather(): from_left = lax.ppermute(from_left, axis, right)]
    pallas_call x0 -> x1, Pallas kernels: none -> 17.9 us  [block_products(): pl.pallas_call(functools.partial(block_kernel, n_grad), out_shape=jax.Sha...]
    dot_general x1 -> x0, matrix products: 8.1 us -> none  [block_products(): jnp.einsum('nbi,nbj->bij', left_rows, right, preferred_element_type=jnp.f...]
    ppermute x0 -> x4, starting transfers between devices: none -> 6.83 us  [the longest x1 2.11 us: ring_gather(): from_left = lax.ppermute(from_left, axis, right)]
  transfers between devices with their start and end apart: 2 -> 5, of which waited for: 2 -> 4; matrix products, arithmetic and copies ran while one was open for 9% -> 2% of each run, Pallas kernels for 0% -> 0%
where the time goes in v1:
time: 140 us
  waiting for transfers between devices  97.1 us (69%)
  Pallas kernels  17.9 us (13%)
  between operations  14.1 us (10%)
  starting transfers between devices  6.83 us (5%)
  local copies, waits for them, and re-layouts  2.99 us (2%)
    all_gather x1, waiting for transfers between devices, on_device(): act_all = lax.all_gather(activations, 'out', axis=0, tiled=True)  66.6 us
    ppermute x1, waiting for transfers between devices, ring_gather(): from_left = lax.ppermute(from_left, axis, right)  20.9 us
    pallas_call x1, Pallas kernels, block_products(): pl.pallas_call(functools.partial(block_kernel, n_grad), out_shape=jax.Sha...  17.9 us
    ppermute x1, waiting for transfers between devices, ring_gather(): near_a = lax.ppermute(from_left[:half], axis, right)  7.33 us
  transfers between devices with their start and end apart: 5, of which 4 were waited for; matrix products, arithmetic and copies ran while one was open for 2% of the time, Pallas kernels for 0%

profile of v1, /device:TPU:1, one launch (start us, length us, event | category | flops | bytes accessed | tf_op | source)
XLA Modules:
  0.0 139.6 jit_solution(16515583925749939865)
XLA Ops:
  6.5 0.0 all-gather.2.cloned.1.call-start
  6.5 0.7 all-gather.2.cloned.1.call-update
  7.3 2.1 %collective-permute-start = (bf16[2048,256]{1,0:T(8,128)(2,1)}, bf16[2048,256]{1,0:T(8,128)(2,1)S(1)}, u32[]{:S(2)}, u32[]{:S(2)}) collective-permute-start(bf16[2048,256]{1,0:T(8,128)(2,1)} %rest_0_.1), channel_id=1, source_target_pairs={{0,64},{64,128},{128,192},{192,0},{1,65},{65,129},{129,193},{193,1... | collective-permute-start | bytes 3145736 | tf_op jit(solution)/shard_map/ppermute | solution.py:85
  9.4 1.4 collective-permute-start.1
  10.7 20.9 %collective-permute-done.rest_1_ = bf16[2048,256]{1,0:T(8,128)(2,1)S(1)} collective-permute-done((bf16[2048,256]{1,0:T(8,128)(2,1)}, bf16[2048,256]{1,0:T(8,128)(2,1)S(1)}, u32[]{:S(2)}, u32[]{:S(2)}) %collective-permute-start) | collective-permute-done | bytes 1048608 | tf_op jit(solution)/shard_map/ppermute | solution.py:85
  31.6 0.8 slice.8
  32.5 1.9 %collective-permute-start.2 = (bf16[1024,256]{1,0:T(8,128)(2,1)}, bf16[1024,256]{1,0:T(8,128)(2,1)S(1)}, u32[]{:S(2)}, u32[]{:S(2)}) collective-permute-start(bf16[1024,256]{1,0:T(8,128)(2,1)} %slice.8), channel_id=1, source_target_pairs={{0,64},{64,128},{128,192},{192,0},{1,65},{65,129},{129,193},{193,1... | collective-permute-start | bytes 1572872 | tf_op jit(solution)/shard_map/ppermute | solution.py:95
  34.3 0.0 collective-permute-done.1.rest_2_
  34.3 0.8 slice.9
  35.2 1.5 %collective-permute-start.3 = (bf16[1024,256]{1,0:T(8,128)(2,1)}, bf16[1024,256]{1,0:T(8,128)(2,1)S(1)}, u32[]{:S(2)}, u32[]{:S(2)}) collective-permute-start(bf16[1024,256]{1,0:T(8,128)(2,1)} %slice.9), channel_id=1, source_target_pairs={{0,192},{64,0},{128,64},{192,128},{1,193},{65,1},{129,65},{193,129... | collective-permute-start | bytes 1572872 | tf_op jit(solution)/shard_map/ppermute | solution.py:96
  37.3 0.1 stack.23.starts_ref
  37.4 0.7 clamp_bitcast_fusion
  38.1 7.3 %collective-permute-done.2.rest_3_ = bf16[1024,256]{1,0:T(8,128)(2,1)S(1)} collective-permute-done((bf16[1024,256]{1,0:T(8,128)(2,1)}, bf16[1024,256]{1,0:T(8,128)(2,1)S(1)}, u32[]{:S(2)}, u32[]{:S(2)}) %collective-permute-start.2) | collective-permute-done | bytes 524320 | tf_op jit(solution)/shard_map/ppermute | solution.py:95
  45.4 1.6 %collective-permute-done.3.rest_4_ = bf16[1024,256]{1,0:T(8,128)(2,1)S(1)} collective-permute-done((bf16[1024,256]{1,0:T(8,128)(2,1)}, bf16[1024,256]{1,0:T(8,128)(2,1)S(1)}, u32[]{:S(2)}, u32[]{:S(2)}) %collective-permute-start.3) | collective-permute-done | bytes 524320 | tf_op jit(solution)/shard_map/ppermute | solution.py:96
  47.0 66.6 %all-gather.2.cloned.1.call-done.act_hbm = bf16[8192,1024]{1,0:T(8,128)(2,1)} async-done(((bf16[128,1024]{1,0:T(8,128)(2,1)}), bf16[8192,1024]{1,0:T(8,128)(2,1)}) %all-gather.2.cloned.1.call-update) | async-done | bytes 16777232 | tf_op jit(solution)/shard_map/all_gather | solution.py:111
  113.6 0.0 copy-start
  113.6 1.2 copy-done
  114.8 17.9 %shard_map.55 = f32[4,128,128]{2,1,0:T(8,128)} custom-call(s32[4]{0:T(128)S(1)} %get-tuple-element.6.rows_ref, s32[4]{0:T(128)S(1)} %get-tuple-element.5.cols_ref, s32[1]{0:T(128)} %bitcast.11.live_ref, s32[5]{0:T(128)S(1)} %stack.23.starts_ref, bf16[8192,1024]{1,0:T(8,128)(2,1)} %all-gather.2.cloned.1.call-done.act_hbm, bf16[2048,256]{1,0:T(8,128)(2,1)S(1)} %copy-done, ...), custom_call_target="tpu_custom_call" | custom-call | flops 1073741824 | bytes 17039360 | tf_op jit(solution)/shard_map/pallas_call | solution.py:62
Async XLA Ops:
  6.5 107.1 %all-gather.2.cloned.1.call-start = ((), (), s32[]{:S(2)}) async-start(), calls=%async_computation | async-start | bytes 17039360 | tf_op jit(solution)/shard_map/all_gather | solution.py:111
  7.3 24.4 %collective-permute-start = (bf16[2048,256]{1,0:T(8,128)(2,1)}, bf16[2048,256]{1,0:T(8,128)(2,1)S(1)}, u32[]{:S(2)}, u32[]{:S(2)}) collective-permute-start(bf16[2048,256]{1,0:T(8,128)(2,1)} %rest_0_.1), channel_id=1, source_target_pairs={{0,64},{64,128},{128,192},{192,0},{1,65},{65,129},{129,193},{193,1... | collective-permute-start | bytes 3145736 | tf_op jit(solution)/shard_map/ppermute | solution.py:85
  9.4 25.0 %collective-permute-start.1 = (bf16[2048,256]{1,0:T(8,128)(2,1)}, bf16[2048,256]{1,0:T(8,128)(2,1)S(1)}, u32[]{:S(2)}, u32[]{:S(2)}) collective-permute-start(bf16[2048,256]{1,0:T(8,128)(2,1)} %rest_0_.1), channel_id=1, source_target_pairs={{0,192},{64,0},{128,64},{192,128},{1,193},{65,1},{129,65},{193,129... | collective-permute-start | bytes 3145736 | tf_op jit(solution)/shard_map/ppermute | solution.py:86
  32.5 12.9 %collective-permute-start.2 = (bf16[1024,256]{1,0:T(8,128)(2,1)}, bf16[1024,256]{1,0:T(8,128)(2,1)S(1)}, u32[]{:S(2)}, u32[]{:S(2)}) collective-permute-start(bf16[1024,256]{1,0:T(8,128)(2,1)} %slice.8), channel_id=1, source_target_pairs={{0,64},{64,128},{128,192},{192,0},{1,65},{65,129},{129,193},{193,1... | collective-permute-start | bytes 1572872 | tf_op jit(solution)/shard_map/ppermute | solution.py:95
  35.2 11.9 %collective-permute-start.3 = (bf16[1024,256]{1,0:T(8,128)(2,1)}, bf16[1024,256]{1,0:T(8,128)(2,1)S(1)}, u32[]{:S(2)}, u32[]{:S(2)}) collective-permute-start(bf16[1024,256]{1,0:T(8,128)(2,1)} %slice.9), channel_id=1, source_target_pairs={{0,192},{64,0},{128,64},{192,128},{1,193},{65,1},{129,65},{193,129... | collective-permute-start | bytes 1572872 | tf_op jit(solution)/shard_map/ppermute | solution.py:96
  113.6 1.2 copy-start
Sparse Core Ops, SparseCore 0:
  10.1 103.4 all-gather.1
